TPU v7x, 32 devices: a whole 2x2x4 slice. The times are simulated.
32 devices in a mesh: grp: 1, node: 8 (over z, y), dev: 4 (over x, core).
Axes of the slice: x: 2, y: 2, z: 4, core: 2. Of those that a mesh axis runs over, the one named last changes fastest.
Arguments:
- query_latent: bfloat16 [32, 128, 512], P(('grp', 'node', 'dev')), may hold values from -35 to 35
- query_rope: bfloat16 [32, 8192], P(('grp', 'node', 'dev')), may hold values from -5 to 5
- latent_cache: bfloat16 [32, 256, 512], P(('grp', 'node', 'dev')), may hold values from -5 to 5
- rope_cache: bfloat16 [32, 64, 256], P(('grp', 'node', 'dev')), may hold values from -5 to 5
- lengths: int32 [32], P(('grp', 'node', 'dev')), may hold values from 2 to 256, as said below
- moe_input: bfloat16 [32, 7168], P(('grp', 'node', 'dev')), may hold values from -6 to 6
- routes: int32 [32, 8], P(('grp', 'node', 'dev')), may hold values from 0 to 15, all different within a row; in each aligned block of 4 rows (0 to 3, 4 to 7, ...) at most 2 rows name the same one
- route_weight: bfloat16 [32, 8], P(('grp', 'node', 'dev')), may hold values from 0.029907227 to 0.29882812
- gate_weight: bfloat16 [32, 7168, 1024], P(('node', 'dev')), may hold values from -0.0625 to 0.0625
- up_weight: bfloat16 [32, 7168, 1024], P(('node', 'dev')), may hold values from -0.0625 to 0.0625
- down_weight: bfloat16 [32, 1024, 7168], P(('node', 'dev')), may hold values from -0.125 to 0.125
Outputs:
- attended: bfloat16 [32, 128, 512], P(('grp', 'node', 'dev'))
- moe_output: bfloat16 [32, 7168], P(('grp', 'node', 'dev'))
Inputs may be any that keep to these rules, and one draw needn't show every extreme that they name: `routes`: each row names 8 different experts; in each aligned block of 4 rows every expert is named by exactly 2 rows. `lengths`: every request has at least two live positions; in every draw some request has all 256.
All inputs are finite; a program needn't handle non-finite values.
Results may differ from a plain program's by a relative error of at most 0.0085.
Values may be sent and summed in bfloat16 or wider, within the bound.
No kernel may reach another device: no remote copies, remote signals or barrier semaphores. Data moves between devices by JAX's collectives and lax.ppermute only.
A program may use at most 128 MiB of HBM per device.

v0:
```python
import math
import jax
import jax.numpy as jnp
from jax import lax
from jax.sharding import PartitionSpec as P

E_NODE = 2
score_scale = 1.0 / math.sqrt(192.0)


def attention_scores(query_latent, rope_query, latent_block, rope_block):
    latent_part = jnp.einsum(
        "rhc,rtc->rht", query_latent, latent_block, preferred_element_type=jnp.float32
    )
    rope_part = jnp.einsum(
        "rhk,rkt->rht", rope_query, rope_block, preferred_element_type=jnp.float32
    )
    return score_scale * (latent_part + rope_part)


def normalize(scores, usable):
    masked = jnp.where(usable, scores, -jnp.inf)
    largest = jnp.max(masked, axis=-1, keepdims=True)
    powers = jnp.exp(masked - largest)
    return (powers / jnp.sum(powers, axis=-1, keepdims=True)).astype(jnp.bfloat16)


def attend(query_latent, query_rope, latent_cache, rope_cache, lengths):
    requests, head_count, latent = query_latent.shape
    context = latent_cache.shape[1]
    rope_query = query_rope.reshape(requests, head_count, -1)
    position = lax.broadcasted_iota(jnp.int32, (1, 1, context), 2)
    usable = position < lengths[:, None, None]
    block_width = min(128, context)
    blocks_live = (jnp.max(lengths) + block_width - 1) // block_width

    def score_block(counter, scores):
        block_start = counter * block_width
        latent_block = lax.dynamic_slice_in_dim(latent_cache, block_start, block_width, 1)
        rope_block = lax.dynamic_slice_in_dim(rope_cache, block_start, block_width, 2)
        block_scores = attention_scores(query_latent, rope_query, latent_block, rope_block)
        return lax.dynamic_update_slice_in_dim(scores, block_scores, block_start, 2)

    empty_scores = jnp.full((requests, head_count, context), -jnp.inf, jnp.float32)
    scores = lax.fori_loop(0, blocks_live, score_block, empty_scores)
    weights = normalize(scores, usable)

    def value_block(counter, accumulated):
        block_start = counter * block_width
        weight_block = lax.dynamic_slice_in_dim(weights, block_start, block_width, 2)
        latent_block = lax.dynamic_slice_in_dim(latent_cache, block_start, block_width, 1)
        return accumulated + jnp.einsum(
            "rht,rtc->rhc", weight_block, latent_block, preferred_element_type=jnp.float32
        )

    output = lax.fori_loop(
        0, blocks_live, value_block, jnp.zeros((requests, head_count, latent), jnp.float32)
    )
    return output.astype(jnp.bfloat16)


def shards(
    query_latent,
    query_rope,
    latent_cache,
    rope_cache,
    lengths,
    moe_input,
    routes,
    route_weight,
    gate_weight,
    up_weight,
    down_weight,
):
    attended = attend(query_latent, query_rope, latent_cache, rope_cache, lengths)
    feature_count = moe_input.shape[1]
    top = routes.shape[1]
    packed = jnp.concatenate(
        [moe_input, routes.astype(jnp.bfloat16), route_weight.astype(jnp.bfloat16)], axis=1
    )
    pool = lax.all_gather(packed, "dev", axis=0, tiled=True)
    pool_rows = pool[:, :feature_count]
    pool_routes = pool[:, feature_count : feature_count + top].astype(jnp.int32)
    pool_weights = pool[:, feature_count + top :]
    node_count = lax.axis_size("node")
    dev_count = lax.axis_size("dev")
    expert_half = lax.axis_index("dev") // (dev_count // E_NODE)
    pooled = pool_rows.shape[0]
    slot_count = pooled * pool_routes.shape[1] // (E_NODE * node_count)
    targets = jnp.arange(node_count, dtype=jnp.int32) * E_NODE + expert_half
    matches = pool_routes[:, :, None] == targets[None, None, :]
    chosen = jnp.sum(matches.astype(jnp.int32), axis=1)
    route_share = jnp.sum(
        jnp.where(matches, pool_weights[:, :, None].astype(jnp.float32), 0.0), axis=1
    )
    before = jnp.cumsum(chosen, axis=0) - chosen
    copies = 1
    per_copy = slot_count // copies
    slot_index = jnp.arange(slot_count, dtype=jnp.int32).reshape(1, copies, per_copy, 1)
    selection = (chosen.T[:, None, None, :] == 1) & (before.T[:, None, None, :] == slot_index)
    selector = selection.astype(jnp.bfloat16)
    weighted = (selection.astype(jnp.float32) * route_share.T[:, None, None, :]).astype(
        jnp.bfloat16
    )
    outgoing = jnp.einsum("ncsp,pd->cnsd", selector, pool_rows, preferred_element_type=jnp.float32)
    outgoing = outgoing.astype(jnp.bfloat16).reshape(copies * node_count, per_copy, feature_count)
    weighted, outgoing = (weighted, outgoing)
    arrived = lax.all_to_all(outgoing, "node", split_axis=0, concat_axis=0, tiled=True)
    peer_count, slot_total, width_total = arrived.shape
    flattened = arrived.reshape(peer_count * slot_total, width_total)
    gate_sum = jnp.dot(flattened, gate_weight[0], preferred_element_type=jnp.float32)
    up_sum = jnp.dot(flattened, up_weight[0], preferred_element_type=jnp.float32)
    hidden = (jax.nn.silu(gate_sum) * up_sum).astype(jnp.bfloat16)
    produced = jnp.dot(hidden, down_weight[0], preferred_element_type=jnp.float32).astype(
        jnp.bfloat16
    )
    partial_value = produced.reshape(peer_count, slot_total, width_total)
    returned = lax.all_to_all(partial_value, "node", split_axis=0, concat_axis=0, tiled=True)
    returned = returned.reshape(copies, node_count, slot_count // copies, feature_count)
    pool_sum = jnp.einsum("ncsp,cnsd->pd", weighted, returned, preferred_element_type=jnp.float32)
    if dev_count > 8:
        combined = lax.psum_scatter(pool_sum, "dev", scatter_dimension=0, tiled=True)
        return (attended, combined.astype(jnp.bfloat16))
    own = lax.axis_index("dev")
    rows_per = pooled // dev_count
    combined = lax.dynamic_slice_in_dim(pool_sum, own * rows_per, rows_per, 0)
    for shift in range(1, dev_count):
        target = (own + shift) % dev_count
        outgoing_part = lax.dynamic_slice_in_dim(pool_sum, target * rows_per, rows_per, 0)
        combined = combined + lax.ppermute(
            outgoing_part, "dev", [(i, (i + shift) % dev_count) for i in range(dev_count)]
        )
    return (attended, combined.astype(jnp.bfloat16))


def solution(mesh):
    in_specs = (
        P(("grp", "node", "dev"), None, None),
        P(("grp", "node", "dev"), None),
        P(("grp", "node", "dev"), None, None),
        P(("grp", "node", "dev"), None, None),
        P(("grp", "node", "dev")),
        P(("grp", "node", "dev"), None),
        P(("grp", "node", "dev"), None),
        P(("grp", "node", "dev"), None),
        P(("node", "dev"), None, None),
        P(("node", "dev"), None, None),
        P(("node", "dev"), None, None),
    )
    out_specs = (P(("grp", "node", "dev"), None, None), P(("grp", "node", "dev"), None))
    return jax.shard_map(shards, mesh=mesh, in_specs=in_specs, out_specs=out_specs, check_vma=False)
```

profile of v0, /device:TPU:0, one launch (start us, length us, event | category | flops | bytes accessed | tf_op | source)
XLA Modules:
  0.0 65.0 jit_solution(8729867085943102680)
XLA Ops:
  0.7 0.7 %convert_element_type.47 = bf16[1,8]{1,0:T(2,128)(2,1)S(1)} convert(s32[1,8]{1,0:T(1,128)} %param.21) | non-fusion elementwise | flops 8 | bytes 48 | tf_op jit(solution)/shard_map/convert_element_type | solution.py:79
  1.3 0.9 %concatenate.3 = bf16[1,7184]{1,0:T(2,128)(2,1)S(1)} concatenate(bf16[1,7168]{1,0:T(2,128)(2,1)} %param.20, bf16[1,8]{1,0:T(2,128)(2,1)S(1)} %convert_element_type.47, bf16[1,8]{1,0:T(2,128)(2,1)} %param.22), dimensions={1} | concatenate | bytes 28736 | tf_op jit(solution)/shard_map/concatenate | solution.py:78
  2.2 6.4 %all-gather = bf16[4,1,7184]{2,1,0:T(2,128)(2,1)S(1)} all-gather(bf16[1,1,7184]{2,1,0:T(2,128)(2,1)S(1)} %bitcast.86), channel_id=1, replica_groups=mesh['grp'=1,'node'=8,'dev'=4] {'dev'}, dimensions={0}, use_global_device_ids=true | all-gather | bytes 71840 | tf_op jit(solution)/shard_map/all_gather | solution.py:81
  8.6 0.1 slice_convert_fusion
  8.7 0.1 fusion.43
  8.8 0.3 fusion.26
  9.1 0.9 %copy.30 = bf16[8,2,7168]{2,1,0:T(2,128)(2,1)} copy(bf16[8,2,7168]{2,0,1:T(8,128)(2,1)S(1)} %fusion.26) | data formatting | bytes 458752 | tf_op jit(solution)/shard_map/reshape | solution.py:106
  10.0 6.3 %all-to-all-start = ((bf16[8,2,7168]{2,1,0:T(2,128)(2,1)}), bf16[8,2,7168]{2,1,0:T(2,128)(2,1)S(1)}, u32[]{:S(2)}, u32[]{:S(2)}) async-start(bf16[8,2,7168]{2,1,0:T(2,128)(2,1)} %copy.30), calls=%async_computation | async-start | bytes 458752 | tf_op jit(solution)/shard_map/all_to_all | solution.py:108
  16.9 0.8 %reduce.2 = bf16[8192]{0:T(1024)(128)(2,1)S(1)} reduce(bf16[1,8192]{1,0:T(2,128)(2,1)} %param.16, bf16[]{:T(256)} %constant.100), dimensions={0}, to_apply=%param.16.reduce_sub_computation | reduce | bytes 32770 | tf_op args[1]
  17.8 0.1 reshape.91
  17.9 2.2 %while.20 = (s32[]{:T(128)}, f32[1,128,256]{2,1,0:T(8,128)S(1)}, s32[]{:T(128)}, bf16[1,256,512]{2,1,0:T(8,128)(2,1)}, bf16[1,128,512]{2,1,0:T(8,128)(2,1)}, /*i...) while((s32[]{:T(128)}, f32[1,128,256]{2,1,0:T(8,128)S(1)}, ...), condition=%wide.region_1.2_spmd, body=%wide.region_0.0_spmd.sunk | while | flops 18907140 | bytes 753831 | solution.py:45
  17.9 1.2 %fusion.70 = f32[128,128]{1,0:T(8,128)S(1)} fusion(bf16[1,128,512]{2,1,0:T(8,128)(2,1)} %get-tuple-element.236, bf16[1,256,512]{2,1,0:T(8,128)(2,1)} %get-tuple-element.235, s32[]{:T(128)S(6)} %select_n.73), kind=kOutput, calls=%fused_computation.3.clone.1 | convolution fusion | flops 16777216 | bytes 327684 | tf_op jit(solution)/shard_map/while/body/rhc,rtc->rht/dot_general | solution.py:12
  19.1 0.9 %fusion.71 = f32[1,128,128]{1,2,0:T(8,128)S(1)} fusion(f32[128,128]{1,0:T(8,128)S(1)} %fusion.70, bf16[1,128,64]{2,1,0:T(8,128)(2,1)S(1)} %get-tuple-element.238, bf16[1,64,256]{2,1,0:T(8,128)(2,1)} %get-tuple-element.237, s32[]{:T(128)S(6)} %select_n.73), kind=kOutput, calls=%fused_computation.2.clone.1 | convolution fusion | flops 2129920 | bytes 163844 | tf_op jit(solution)/shard_map/while/body/rhk,rkt->rht/dot_general | solution.py:15
  20.0 0.1 copy.41
  20.1 0.1 select_reduce_fusion
  20.2 5.0 %all-to-all-done = bf16[8,2,7168]{2,1,0:T(2,128)(2,1)S(1)} async-done(((bf16[8,2,7168]{2,1,0:T(2,128)(2,1)}), bf16[8,2,7168]{2,1,0:T(2,128)(2,1)S(1)}, u32[]{:S(2)}, u32[]{:S(2)}) %all-to-all-start) | async-done | bytes 229408 | tf_op jit(solution)/shard_map/all_to_all | solution.py:108
  25.2 0.1 reshape.93
  25.3 7.2 %fusion.21 = f32[16,1024]{1,0:T(8,128)S(1)} fusion(bf16[16,7168]{1,0:T(8,128)(2,1)S(1)} %reshape.93, bf16[1,7168,1024]{2,1,0:T(8,128)(2,1)} %param.23), kind=kOutput, calls=%fused_computation.24 | convolution fusion | flops 234881024 | bytes 14974976 | tf_op jit(solution)/shard_map/dot_general | solution.py:111
  32.5 0.0 copy-start
  32.5 13.3 %fusion.23 = bf16[16,7168]{1,0:T(8,128)(2,1)S(1)} fusion(bf16[1,1024,7168]{2,1,0:T(8,128)(2,1)} %param.25, bf16[16,7168]{1,0:T(8,128)(2,1)S(1)} %reshape.93, bf16[1,7168,1024]{2,1,0:T(8,128)(2,1)} %param.24, f32[16,1024]{1,0:T(8,128)S(1)} %fusion.21), kind=kOutput, calls=%fused_computation.27 | convolution fusion | flops 469975040 | bytes 29884416 | tf_op jit(solution)/shard_map/dot_general | solution.py:114
  45.8 0.8 %reshape.94 = bf16[8,2,7168]{2,1,0:T(2,128)(2,1)} reshape(bf16[16,7168]{1,0:T(8,128)(2,1)S(1)} %fusion.23) | data formatting | bytes 458752 | tf_op jit(solution)/shard_map/reshape | solution.py:117
  46.6 3.4 %all-to-all-start.1 = ((bf16[8,2,7168]{2,1,0:T(2,128)(2,1)}), bf16[8,2,7168]{2,1,0:T(2,128)(2,1)S(1)}, u32[]{:S(2)}, u32[]{:S(2)}) async-start(bf16[8,2,7168]{2,1,0:T(2,128)(2,1)} %reshape.94), calls=%async_computation.1 | async-start | bytes 458752 | tf_op jit(solution)/shard_map/all_to_all | solution.py:118
  50.0 0.1 fusion.44
  50.1 0.2 fusion.36
  50.3 0.1 divide_convert_fusion
  50.4 7.9 %all-to-all-done.1 = bf16[8,2,7168]{2,1,0:T(2,128)(2,1)S(1)} async-done(((bf16[8,2,7168]{2,1,0:T(2,128)(2,1)}), bf16[8,2,7168]{2,1,0:T(2,128)(2,1)S(1)}, u32[]{:S(2)}, u32[]{:S(2)}) %all-to-all-start.1) | async-done | bytes 229408 | tf_op jit(solution)/shard_map/all_to_all | solution.py:118
  58.4 0.2 convolution_bitcast_fusion.1
  58.6 0.1 constant_dynamic-slice_fusion.2
  58.7 0.1 collective-permute-start
  58.7 1.7 %collective-permute-start.2 = (f32[1,7168]{1,0:T(1,128)S(1)}, f32[1,7168]{1,0:T(1,128)S(1)}, u32[]{:S(2)}, u32[]{:S(2)}) collective-permute-start(f32[1,7168]{1,0:T(1,128)S(1)} %get-tuple-element.130), channel_id=1, source_target_pairs={{0,3},{1,0},{2,1},{3,2},{4,7},{5,4},{6,5},{7,6},{8,11},{9,8},{10,9... | collective-permute-start | bytes 86024 | tf_op jit(solution)/shard_map/ppermute | solution.py:130
  60.5 1.5 %collective-permute-start.1 = (f32[1,7168]{1,0:T(1,128)S(1)}, f32[1,7168]{1,0:T(1,128)S(1)}, u32[]{:S(2)}, u32[]{:S(2)}) collective-permute-start(f32[1,7168]{1,0:T(1,128)S(1)} %get-tuple-element.131), channel_id=1, source_target_pairs={{0,2},{1,3},{2,0},{3,1},{4,6},{5,7},{6,4},{7,5},{8,10},{9,11},{10,... | collective-permute-start | bytes 86024 | tf_op jit(solution)/shard_map/ppermute | solution.py:130
  62.0 0.0 copy-done
  62.0 0.2 while.21
  62.0 0.2 fusion.74
  62.2 0.7 %convert_element_type.46 = bf16[1,128,512]{2,1,0:T(8,128)(2,1)} convert(f32[1,128,512]{2,1,0:T(8,128)S(1)} %get-tuple-element.69) | non-fusion elementwise | flops 65536 | bytes 393216 | tf_op jit(solution)/shard_map/convert_element_type | solution.py:59
  62.9 0.0 collective-permute-done
  62.9 0.0 collective-permute-done.2
  62.9 1.4 %collective-permute-done.1 = f32[1,7168]{1,0:T(1,128)S(1)} collective-permute-done((f32[1,7168]{1,0:T(1,128)S(1)}, f32[1,7168]{1,0:T(1,128)S(1)}, u32[]{:S(2)}, u32[]{:S(2)}) %collective-permute-start.1) | collective-permute-done | bytes 28704 | tf_op jit(solution)/shard_map/ppermute | solution.py:130
  64.4 0.7 %add_convert_fusion = bf16[1,7168]{1,0:T(2,128)(2,1)} fusion(f32[1,7168]{1,0:T(1,128)S(1)} %collective-permute-done.2, f32[1,7168]{1,0:T(1,128)S(1)} %collective-permute-done.1, f32[1,7168]{1,0:T(1,128)S(1)} %collective-permute-done, f32[4,7168]{1,0:T(4,128)S(1)} %convolution_bitcast_fusion.1, s32[]{:T(128)S(6)} %select_n.55), kind=kLoop, calls=%fused_computation.45 | loop fusion | flops 28672 | bytes 129028 | tf_op jit(solution)/shard_map/convert_element_type | solution.py:133
  (9 shorter events, 0.1 us)
Async XLA Ops:
  10.0 15.2 %all-to-all-start = ((bf16[8,2,7168]{2,1,0:T(2,128)(2,1)}), bf16[8,2,7168]{2,1,0:T(2,128)(2,1)S(1)}, u32[]{:S(2)}, u32[]{:S(2)}) async-start(bf16[8,2,7168]{2,1,0:T(2,128)(2,1)} %copy.30), calls=%async_computation | async-start | bytes 458752 | tf_op jit(solution)/shard_map/all_to_all | solution.py:108
  32.5 29.5 %copy-start = (bf16[1,256,512]{2,1,0:T(8,128)(2,1)S(1)}, bf16[1,256,512]{2,1,0:T(8,128)(2,1)}, u32[]{:S(2)}) copy-start(bf16[1,256,512]{2,1,0:T(8,128)(2,1)} %get-tuple-element.270) | copy-start | bytes 786436
  46.6 11.8 %all-to-all-start.1 = ((bf16[8,2,7168]{2,1,0:T(2,128)(2,1)}), bf16[8,2,7168]{2,1,0:T(2,128)(2,1)S(1)}, u32[]{:S(2)}, u32[]{:S(2)}) async-start(bf16[8,2,7168]{2,1,0:T(2,128)(2,1)} %reshape.94), calls=%async_computation.1 | async-start | bytes 458752 | tf_op jit(solution)/shard_map/all_to_all | solution.py:118
  58.7 4.2 %collective-permute-start = (f32[1,7168]{1,0:T(1,128)S(1)}, f32[1,7168]{1,0:T(1,128)S(1)}, u32[]{:S(2)}, u32[]{:S(2)}) collective-permute-start(f32[1,7168]{1,0:T(1,128)S(1)} %get-tuple-element.129), channel_id=1, source_target_pairs={{0,1},{1,2},{2,3},{3,0},{4,5},{5,6},{6,7},{7,4},{8,9},{9,10},{10,1... | collective-permute-start | bytes 86024 | tf_op jit(solution)/shard_map/ppermute | solution.py:130
  58.7 4.2 %collective-permute-start.2 = (f32[1,7168]{1,0:T(1,128)S(1)}, f32[1,7168]{1,0:T(1,128)S(1)}, u32[]{:S(2)}, u32[]{:S(2)}) collective-permute-start(f32[1,7168]{1,0:T(1,128)S(1)} %get-tuple-element.130), channel_id=1, source_target_pairs={{0,3},{1,0},{2,1},{3,2},{4,7},{5,4},{6,5},{7,6},{8,11},{9,8},{10,9... | collective-permute-start | bytes 86024 | tf_op jit(solution)/shard_map/ppermute | solution.py:130
  60.5 3.9 %collective-permute-start.1 = (f32[1,7168]{1,0:T(1,128)S(1)}, f32[1,7168]{1,0:T(1,128)S(1)}, u32[]{:S(2)}, u32[]{:S(2)}) collective-permute-start(f32[1,7168]{1,0:T(1,128)S(1)} %get-tuple-element.131), channel_id=1, source_target_pairs={{0,2},{1,3},{2,0},{3,1},{4,6},{5,7},{6,4},{7,5},{8,10},{9,11},{10,... | collective-permute-start | bytes 86024 | tf_op jit(solution)/shard_map/ppermute | solution.py:130
where the time goes:
time: 65.6 us; the launch traced here: 65 us
  matrix products  23.2 us (35%)
  waiting for transfers between devices  14.3 us (22%)
  starting transfers between devices  12.9 us (20%)
  blocking collectives  6.39 us (10%)
  other arithmetic  3.57 us (5%)
  local copies, waits for them, and re-layouts  2.96 us (5%)
  between operations  1.47 us (2%)
    dot_general x1, matrix products, shards(): jnp.dot(hidden, down_weight[0], preferred_element_type=jnp.float32)  13.3 us
    all_to_all x1, waiting for transfers between devices, shards(): lax.all_to_all(partial_value, 'node', split_axis=0, concat_axis=0, tiled=...  7.94 us
    dot_general x1, matrix products, shards(): jnp.dot(flattened, gate_weight[0], preferred_element_type=jnp.float32)  7.17 us
    all_gather x1, blocking collectives, shards(): pool = lax.all_gather(packed, 'dev', axis=0, tiled=True)  6.39 us
    all_to_all x1, starting transfers between devices, shards(): lax.all_to_all(outgoing, 'node', split_axis=0, concat_axis=0, tiled=True)  6.26 us
    all_to_all x1, waiting for transfers between devices, shards(): lax.all_to_all(outgoing, 'node', split_axis=0, concat_axis=0, tiled=True)  4.97 us
    all_to_all x1, starting transfers between devices, shards(): lax.all_to_all(partial_value, 'node', split_axis=0, concat_axis=0, tiled=...  3.4 us
    ppermute x3, starting transfers between devices, shards(): lax.ppermute(outgoing_part, 'dev', [(i, (i + shift) % dev_count) for i in...  3.28 us
  transfers between devices with their start and end apart: 5, of which 3 were waited for; matrix products, arithmetic and copies ran while one was open for 7% of the time, Pallas kernels for 0%

commit v1 on v0

--- a/solution.py
+++ b/solution.py
@@ -1,11 +1,27 @@
+import functools
 import math
 import jax
 import jax.numpy as jnp
 from jax import lax
 from jax.sharding import PartitionSpec as P
+from jax.lax import axis_index, axis_size, ppermute
 
 E_NODE = 2
 score_scale = 1.0 / math.sqrt(192.0)
+
+
+def _write_streams(field, dim_no):
+    n_chips = axis_size("dev")
+    fields = [(to_i, (to_i + 1) % n_chips) for to_i in range(n_chips)]
+    ready = [None] * n_chips
+    ready[n_chips - 1] = field
+    for m in range(n_chips - 2, -1, -1):
+        ready[m] = ppermute(ready[m + 1], perm=fields, axis_name="dev")
+    wide_out = jnp.concatenate(ready, dim_no)
+    return jnp.roll(wide_out, (axis_index("dev") + 1) * field.shape[dim_no], dim_no)
+
+
+connect_terms = functools.partial(_write_streams, dim_no=0)
 
 
 def attention_scores(query_latent, rope_query, latent_block, rope_block):
@@ -78,7 +94,7 @@
     packed = jnp.concatenate(
         [moe_input, routes.astype(jnp.bfloat16), route_weight.astype(jnp.bfloat16)], axis=1
     )
-    pool = lax.all_gather(packed, "dev", axis=0, tiled=True)
+    pool = connect_terms(packed)
     pool_rows = pool[:, :feature_count]
     pool_routes = pool[:, feature_count : feature_count + top].astype(jnp.int32)
     pool_weights = pool[:, feature_count + top :]

time: 65.6 us -> 69.8 us (1.064)
  waiting for transfers between devices: 14.3 us -> 24.2 us
  blocking collectives: 6.39 us -> 0 us
    ppermute x0 -> x3, waiting for transfers between devices: none -> 8.26 us  [_write_streams(): ready[m] = ppermute(ready[m + 1], perm=fields, axis_name='dev')]
    all_gather x1 -> x0, blocking collectives: 6.39 us -> none  [shards(): pool = lax.all_gather(packed, 'dev', axis=0, tiled=True)]
    all_to_all x1, waiting for transfers between devices: 4.97 us -> 6.17 us  [shards(): lax.all_to_all(outgoing, 'node', split_axis=0, concat_axis=0, tiled=True)]
  transfers between devices with their start and end apart: 5 -> 8, of which waited for: 3 -> 6; matrix products, arithmetic and copies ran while one was open for 7% -> 6% of each run, Pallas kernels for 0% -> 0%
where the time goes in v1:
time: 69.8 us; the launch traced here: 69.2 us
  waiting for transfers between devices  24.2 us (35%)
  matrix products  23.2 us (33%)
  starting transfers between devices  13.3 us (19%)
  other arithmetic  3.58 us (5%)
  local copies, waits for them, and re-layouts  3.28 us (5%)
  between operations  1.46 us (2%)
    dot_general x1, matrix products, shards(): jnp.dot(hidden, down_weight[0], preferred_element_type=jnp.float32)  13.3 us
    ppermute x3, waiting for transfers between devices, _write_streams(): ready[m] = ppermute(ready[m + 1], perm=fields, axis_name='dev')  8.26 us
    all_to_all x1, waiting for transfers between devices, shards(): lax.all_to_all(partial_value, 'node', split_axis=0, concat_axis=0, tiled=...  7.66 us
    dot_general x1, matrix products, shards(): jnp.dot(flattened, gate_weight[0], preferred_element_type=jnp.float32)  7.17 us
    all_to_all x1, starting transfers between devices, shards(): lax.all_to_all(outgoing, 'node', split_axis=0, concat_axis=0, tiled=True)  6.64 us
    all_to_all x1, waiting for transfers between devices, shards(): lax.all_to_all(outgoing, 'node', split_axis=0, concat_axis=0, tiled=True)  6.17 us
    all_to_all x1, starting transfers between devices, shards(): lax.all_to_all(partial_value, 'node', split_axis=0, concat_axis=0, tiled=...  3.4 us
    ppermute x3, starting transfers between devices, shards(): lax.ppermute(outgoing_part, 'dev', [(i, (i + shift) % dev_count) for i in...  2.6 us
  transfers between devices with their start and end apart: 8, of which 6 were waited for; matrix products, arithmetic and copies ran while one was open for 6% of the time, Pallas kernels for 0%

profile of v1, /device:TPU:0, one launch (start us, length us, event | category | flops | bytes accessed | tf_op | source)
XLA Modules:
  0.0 69.2 jit_solution(14331962154739163052)
XLA Ops:
  0.6 0.7 convert_element_type.47
  1.3 0.9 %concatenate.9 = bf16[1,7184]{1,0:T(2,128)(2,1)S(1)} concatenate(bf16[1,7168]{1,0:T(2,128)(2,1)} %param.20, bf16[1,8]{1,0:T(2,128)(2,1)S(1)} %convert_element_type.47, bf16[1,8]{1,0:T(2,128)(2,1)} %param.22), dimensions={1} | concatenate | bytes 28736 | tf_op jit(solution)/shard_map/concatenate | solution.py:94
  2.2 0.5 collective-permute-start
  2.6 3.5 %collective-permute-done = bf16[1,7184]{1,0:T(2,128)(2,1)S(1)} collective-permute-done((bf16[1,7184]{1,0:T(2,128)(2,1)S(1)}, bf16[1,7184]{1,0:T(2,128)(2,1)S(1)}, u32[]{:S(2)}, u32[]{:S(2)}) %collective-permute-start) | collective-permute-done | bytes 14400 | tf_op jit(solution)/shard_map/ppermute | solution.py:19
  6.1 0.1 collective-permute-start.1
  6.2 3.2 %collective-permute-done.1 = bf16[1,7184]{1,0:T(2,128)(2,1)S(1)} collective-permute-done((bf16[1,7184]{1,0:T(2,128)(2,1)S(1)}, bf16[1,7184]{1,0:T(2,128)(2,1)S(1)}, u32[]{:S(2)}, u32[]{:S(2)}) %collective-permute-start.1) | collective-permute-done | bytes 14400 | tf_op jit(solution)/shard_map/ppermute | solution.py:19
  9.4 0.1 collective-permute-start.2
  10.2 0.8 %reduce.2 = bf16[8192]{0:T(1024)(128)(2,1)S(1)} reduce(bf16[1,8192]{1,0:T(2,128)(2,1)} %param.16, bf16[]{:T(256)} %constant.114), dimensions={0}, to_apply=%param.16.reduce_sub_computation | reduce | bytes 32770 | tf_op args[1]
  11.0 0.1 reshape.91
  11.1 1.6 %collective-permute-done.2 = bf16[1,7184]{1,0:T(2,128)(2,1)S(1)} collective-permute-done((bf16[1,7184]{1,0:T(2,128)(2,1)S(1)}, bf16[1,7184]{1,0:T(2,128)(2,1)S(1)}, u32[]{:S(2)}, u32[]{:S(2)}) %collective-permute-start.2) | collective-permute-done | bytes 14400 | tf_op jit(solution)/shard_map/ppermute | solution.py:19
  12.7 0.3 concatenate.10
  13.0 0.1 dynamic-slice_convert_fusion
  13.1 0.1 fusion.43
  13.3 0.3 fusion.26
  13.5 0.9 %copy.26 = bf16[8,2,7168]{2,1,0:T(2,128)(2,1)} copy(bf16[8,2,7168]{2,0,1:T(8,128)(2,1)S(1)} %fusion.26) | data formatting | bytes 458752 | tf_op jit(solution)/shard_map/reshape | solution.py:122
  14.5 6.6 %all-to-all-start = ((bf16[8,2,7168]{2,1,0:T(2,128)(2,1)}), bf16[8,2,7168]{2,1,0:T(2,128)(2,1)S(1)}, u32[]{:S(2)}, u32[]{:S(2)}) async-start(bf16[8,2,7168]{2,1,0:T(2,128)(2,1)} %copy.26), calls=%async_computation | async-start | bytes 458752 | tf_op jit(solution)/shard_map/all_to_all | solution.py:124
  21.1 2.2 %while.20 = (s32[]{:T(128)}, f32[1,128,256]{2,1,0:T(8,128)S(1)}, s32[]{:T(128)}, bf16[1,256,512]{2,1,0:T(8,128)(2,1)}, bf16[1,128,512]{2,1,0:T(8,128)(2,1)}, /*i...) while((s32[]{:T(128)}, f32[1,128,256]{2,1,0:T(8,128)S(1)}, ...), condition=%wide.region_1.2_spmd, body=%wide.region_0.0_spmd.sunk | while | flops 18907140 | bytes 753831 | solution.py:61
  21.1 1.2 %fusion.71 = f32[128,128]{1,0:T(8,128)S(1)} fusion(bf16[1,128,512]{2,1,0:T(8,128)(2,1)} %get-tuple-element.229, bf16[1,256,512]{2,1,0:T(8,128)(2,1)} %get-tuple-element.228, s32[]{:T(128)S(6)} %select_n.84), kind=kOutput, calls=%fused_computation.3.clone.1 | convolution fusion | flops 16777216 | bytes 327684 | tf_op jit(solution)/shard_map/while/body/rhc,rtc->rht/dot_general | solution.py:28
  22.3 0.9 %fusion.72 = f32[1,128,128]{1,2,0:T(8,128)S(1)} fusion(f32[128,128]{1,0:T(8,128)S(1)} %fusion.71, bf16[1,128,64]{2,1,0:T(8,128)(2,1)S(1)} %get-tuple-element.231, bf16[1,64,256]{2,1,0:T(8,128)(2,1)} %get-tuple-element.230, s32[]{:T(128)S(6)} %select_n.84), kind=kOutput, calls=%fused_computation.2.clone.1 | convolution fusion | flops 2129920 | bytes 163844 | tf_op jit(solution)/shard_map/while/body/rhk,rkt->rht/dot_general | solution.py:31
  23.2 0.1 copy.34
  23.4 0.1 select_reduce_fusion
  23.5 6.2 %all-to-all-done = bf16[8,2,7168]{2,1,0:T(2,128)(2,1)S(1)} async-done(((bf16[8,2,7168]{2,1,0:T(2,128)(2,1)}), bf16[8,2,7168]{2,1,0:T(2,128)(2,1)S(1)}, u32[]{:S(2)}, u32[]{:S(2)}) %all-to-all-start) | async-done | bytes 229408 | tf_op jit(solution)/shard_map/all_to_all | solution.py:124
  29.6 0.1 reshape.93
  29.7 7.2 %fusion.21 = f32[16,1024]{1,0:T(8,128)S(1)} fusion(bf16[16,7168]{1,0:T(8,128)(2,1)S(1)} %reshape.93, bf16[1,7168,1024]{2,1,0:T(8,128)(2,1)} %param.23), kind=kOutput, calls=%fused_computation.24 | convolution fusion | flops 234881024 | bytes 14974976 | tf_op jit(solution)/shard_map/dot_general | solution.py:127
  36.9 0.0 copy-start
  36.9 13.3 %fusion.23 = bf16[16,7168]{1,0:T(8,128)(2,1)S(1)} fusion(bf16[1,1024,7168]{2,1,0:T(8,128)(2,1)} %param.25, bf16[16,7168]{1,0:T(8,128)(2,1)S(1)} %reshape.93, bf16[1,7168,1024]{2,1,0:T(8,128)(2,1)} %param.24, f32[16,1024]{1,0:T(8,128)S(1)} %fusion.21), kind=kOutput, calls=%fused_computation.27 | convolution fusion | flops 469975040 | bytes 29884416 | tf_op jit(solution)/shard_map/dot_general | solution.py:130
  50.2 0.8 %reshape.94 = bf16[8,2,7168]{2,1,0:T(2,128)(2,1)} reshape(bf16[16,7168]{1,0:T(8,128)(2,1)S(1)} %fusion.23) | data formatting | bytes 458752 | tf_op jit(solution)/shard_map/reshape | solution.py:133
  51.0 3.4 %all-to-all-start.1 = ((bf16[8,2,7168]{2,1,0:T(2,128)(2,1)}), bf16[8,2,7168]{2,1,0:T(2,128)(2,1)S(1)}, u32[]{:S(2)}, u32[]{:S(2)}) async-start(bf16[8,2,7168]{2,1,0:T(2,128)(2,1)} %reshape.94), calls=%async_computation.1 | async-start | bytes 458752 | tf_op jit(solution)/shard_map/all_to_all | solution.py:134
  54.4 0.2 fusion.36
  54.6 0.1 divide_convert_fusion
  54.7 0.1 fusion.44
  54.8 7.7 %all-to-all-done.1 = bf16[8,2,7168]{2,1,0:T(2,128)(2,1)S(1)} async-done(((bf16[8,2,7168]{2,1,0:T(2,128)(2,1)}), bf16[8,2,7168]{2,1,0:T(2,128)(2,1)S(1)}, u32[]{:S(2)}, u32[]{:S(2)}) %all-to-all-start.1) | async-done | bytes 229408 | tf_op jit(solution)/shard_map/all_to_all | solution.py:134
  62.5 0.2 convolution_bitcast_fusion.1
  62.7 0.1 constant_dynamic-slice_fusion.2
  62.8 0.1 collective-permute-start.3
  62.9 1.7 %collective-permute-start.5 = (f32[1,7168]{1,0:T(1,128)S(1)}, f32[1,7168]{1,0:T(1,128)S(1)}, u32[]{:S(2)}, u32[]{:S(2)}) collective-permute-start(f32[1,7168]{1,0:T(1,128)S(1)} %get-tuple-element.125), channel_id=1, source_target_pairs={{0,3},{1,0},{2,1},{3,2},{4,7},{5,4},{6,5},{7,6},{8,11},{9,8},{10,9... | collective-permute-start | bytes 86024 | tf_op jit(solution)/shard_map/ppermute | solution.py:146
  64.6 0.8 %collective-permute-start.4 = (f32[1,7168]{1,0:T(1,128)S(1)}, f32[1,7168]{1,0:T(1,128)S(1)}, u32[]{:S(2)}, u32[]{:S(2)}) collective-permute-start(f32[1,7168]{1,0:T(1,128)S(1)} %get-tuple-element.126), channel_id=1, source_target_pairs={{0,2},{1,3},{2,0},{3,1},{4,6},{5,7},{6,4},{7,5},{8,10},{9,11},{10,... | collective-permute-start | bytes 86024 | tf_op jit(solution)/shard_map/ppermute | solution.py:146
  65.5 0.0 copy-done
  65.5 0.2 while.21
  65.5 0.2 fusion.75
  65.7 0.7 convert_element_type.46
  66.4 0.0 collective-permute-done.3
  66.4 0.0 collective-permute-done.5
  66.4 2.1 %collective-permute-done.4 = f32[1,7168]{1,0:T(1,128)S(1)} collective-permute-done((f32[1,7168]{1,0:T(1,128)S(1)}, f32[1,7168]{1,0:T(1,128)S(1)}, u32[]{:S(2)}, u32[]{:S(2)}) %collective-permute-start.4) | collective-permute-done | bytes 28704 | tf_op jit(solution)/shard_map/ppermute | solution.py:146
  68.5 0.7 add_convert_fusion
  (8 shorter events, 0.1 us)
Async XLA Ops:
  2.2 3.9 %collective-permute-start = (bf16[1,7184]{1,0:T(2,128)(2,1)S(1)}, bf16[1,7184]{1,0:T(2,128)(2,1)S(1)}, u32[]{:S(2)}, u32[]{:S(2)}) collective-permute-start(bf16[1,7184]{1,0:T(2,128)(2,1)S(1)} %concatenate.9), channel_id=1, source_target_pairs={{0,1},{1,2},{2,3},{3,0},{4,5},{5,6},{6,7},{7,4},{8,9},{9,10},{10,1... | collective-permute-start | bytes 43112 | tf_op jit(solution)/shard_map/ppermute | solution.py:19
  6.1 3.3 %collective-permute-start.1 = (bf16[1,7184]{1,0:T(2,128)(2,1)S(1)}, bf16[1,7184]{1,0:T(2,128)(2,1)S(1)}, u32[]{:S(2)}, u32[]{:S(2)}) collective-permute-start(bf16[1,7184]{1,0:T(2,128)(2,1)S(1)} %collective-permute-done), channel_id=1, source_target_pairs={{0,1},{1,2},{2,3},{3,0},{4,5},{5,6},{6,7},{7,4},{8,9},{9,10},{10,1... | collective-permute-start | bytes 43112 | tf_op jit(solution)/shard_map/ppermute | solution.py:19
  9.4 3.3 %collective-permute-start.2 = (bf16[1,7184]{1,0:T(2,128)(2,1)S(1)}, bf16[1,7184]{1,0:T(2,128)(2,1)S(1)}, u32[]{:S(2)}, u32[]{:S(2)}) collective-permute-start(bf16[1,7184]{1,0:T(2,128)(2,1)S(1)} %collective-permute-done.1), channel_id=1, source_target_pairs={{0,1},{1,2},{2,3},{3,0},{4,5},{5,6},{6,7},{7,4},{8,9},{9,10},{10,1... | collective-permute-start | bytes 43112 | tf_op jit(solution)/shard_map/ppermute | solution.py:19
  14.5 15.2 %all-to-all-start = ((bf16[8,2,7168]{2,1,0:T(2,128)(2,1)}), bf16[8,2,7168]{2,1,0:T(2,128)(2,1)S(1)}, u32[]{:S(2)}, u32[]{:S(2)}) async-start(bf16[8,2,7168]{2,1,0:T(2,128)(2,1)} %copy.26), calls=%async_computation | async-start | bytes 458752 | tf_op jit(solution)/shard_map/all_to_all | solution.py:124
  36.9 28.6 %copy-start = (bf16[1,256,512]{2,1,0:T(8,128)(2,1)S(1)}, bf16[1,256,512]{2,1,0:T(8,128)(2,1)}, u32[]{:S(2)}) copy-start(bf16[1,256,512]{2,1,0:T(8,128)(2,1)} %get-tuple-element.263) | copy-start | bytes 786436
  51.0 11.5 %all-to-all-start.1 = ((bf16[8,2,7168]{2,1,0:T(2,128)(2,1)}), bf16[8,2,7168]{2,1,0:T(2,128)(2,1)S(1)}, u32[]{:S(2)}, u32[]{:S(2)}) async-start(bf16[8,2,7168]{2,1,0:T(2,128)(2,1)} %reshape.94), calls=%async_computation.1 | async-start | bytes 458752 | tf_op jit(solution)/shard_map/all_to_all | solution.py:134
  62.8 3.6 %collective-permute-start.3 = (f32[1,7168]{1,0:T(1,128)S(1)}, f32[1,7168]{1,0:T(1,128)S(1)}, u32[]{:S(2)}, u32[]{:S(2)}) collective-permute-start(f32[1,7168]{1,0:T(1,128)S(1)} %get-tuple-element.124), channel_id=1, source_target_pairs={{0,1},{1,2},{2,3},{3,0},{4,5},{5,6},{6,7},{7,4},{8,9},{9,10},{10,1... | collective-permute-start | bytes 86024 | tf_op jit(solution)/shard_map/ppermute | solution.py:146
  62.9 3.5 %collective-permute-start.5 = (f32[1,7168]{1,0:T(1,128)S(1)}, f32[1,7168]{1,0:T(1,128)S(1)}, u32[]{:S(2)}, u32[]{:S(2)}) collective-permute-start(f32[1,7168]{1,0:T(1,128)S(1)} %get-tuple-element.125), channel_id=1, source_target_pairs={{0,3},{1,0},{2,1},{3,2},{4,7},{5,4},{6,5},{7,6},{8,11},{9,8},{10,9... | collective-permute-start | bytes 86024 | tf_op jit(solution)/shard_map/ppermute | solution.py:146
  64.6 3.9 %collective-permute-start.4 = (f32[1,7168]{1,0:T(1,128)S(1)}, f32[1,7168]{1,0:T(1,128)S(1)}, u32[]{:S(2)}, u32[]{:S(2)}) collective-permute-start(f32[1,7168]{1,0:T(1,128)S(1)} %get-tuple-element.126), channel_id=1, source_target_pairs={{0,2},{1,3},{2,0},{3,1},{4,6},{5,7},{6,4},{7,5},{8,10},{9,11},{10,... | collective-permute-start | bytes 86024 | tf_op jit(solution)/shard_map/ppermute | solution.py:146
